TPU v7x, 256 devices: a whole 4x4x8 slice. The times are simulated.
256 devices in a mesh: seq: 4 (over y), ch: 64 (over x, z, core).
Axes of the slice: x: 4, y: 4, z: 8, core: 2. Of those that a mesh axis runs over, the one named last changes fastest.
Arguments:
- tokens: bfloat16 [1024, 8192], P('seq', 'ch'), may hold values from -6 to 6
- in_weight: bfloat16 [8192, 3, 8192], P(None, None, 'ch'), may hold values from -0.0625 to 0.0625
- short_taps: float32 [3, 3, 8192], P(None, None, 'ch'), may hold values from -3 to 3
- decay_rates: float32 [16, 512], P(None, 'ch'), may hold values from 0.05 to 200
- residues: float32 [16, 512], P(None, 'ch'), may hold values from -0.18 to 0.18
- out_weight: bfloat16 [8192, 8192], P('ch'), may hold values from -0.1875 to 0.1875
Outputs:
- mixed: bfloat16 [1024, 8192], P('seq', 'ch')
All inputs are finite; a program needn't handle non-finite values.
Results may differ from a plain program's by a relative error of at most 0.007.
Values may be sent and summed in bfloat16 or wider, within the bound.
No kernel may reach another device: no remote copies, remote signals or barrier semaphores. Data moves between devices by JAX's collectives and lax.ppermute only.
A program may use at most 64 MiB of HBM per device.

v0:
```python
import math
import jax
import jax.numpy as jnp
from jax import lax
from jax.sharding import PartitionSpec as P

TAPS = 3


def passed_along(block, axis, distance):
    devices = range(lax.axis_size(axis))
    route = [(i - distance, i) for i in devices if i - distance in devices]
    return lax.ppermute(block, axis, route)


def on_device(tokens, in_weight, short_taps, decay_rates, residues, out_weight):
    rows_here = tokens.shape[0]
    width_here = in_weight.shape[2]
    model_width = in_weight.shape[0]
    filter_count = decay_rates.shape[1]
    mode_count = decay_rates.shape[0]
    group_width = width_here // filter_count
    tokens_all = rows_here * lax.axis_size("seq")
    flat_weight = in_weight.reshape(model_width, 3 * width_here)
    gathered = lax.all_gather(tokens, "ch", axis=1, tiled=True)
    projected = jnp.dot(gathered, flat_weight, preferred_element_type=jnp.float32).astype(
        jnp.bfloat16
    )
    previous = passed_along(projected[rows_here - (TAPS - 1) :], "seq", 1)
    padded = jnp.concatenate([previous, projected], axis=0).astype(jnp.float32)
    flat_taps = short_taps.reshape(TAPS, 3 * width_here)
    filtered = jnp.zeros((rows_here, 3 * width_here), jnp.float32)
    for shift_back in range(TAPS):
        filtered = (
            filtered
            + flat_taps[shift_back]
            * padded[TAPS - 1 - shift_back : TAPS - 1 - shift_back + rows_here]
        )
    query_stream = filtered[:, :width_here]
    gated_in = filtered[:, width_here : 2 * width_here] * filtered[:, 2 * width_here :]
    block_len = math.gcd(rows_here, 128)
    block_count = rows_here // block_len
    scaled_rates = decay_rates / tokens_all
    offsets_in = jnp.arange(block_len, dtype=jnp.float32)
    filter_taps = jnp.sum(
        residues[None] * jnp.exp(-scaled_rates[None] * offsets_in[:, None, None]), axis=1
    )
    distance = jnp.arange(block_len)[:, None] - jnp.arange(block_len)[None, :]
    lookup = jnp.maximum(distance, 0)
    toeplitz = jnp.where((distance >= 0)[None], filter_taps.T[:, lookup], 0.0)
    blocks_in = gated_in.reshape(block_count, block_len, filter_count, group_width)
    local_part = jnp.einsum("gts,bsgi->btgi", toeplitz, blocks_in, precision=lax.Precision.HIGHEST)
    end_weights = jnp.exp(-scaled_rates[:, :, None] * (block_len - 1 - offsets_in)[None, None, :])
    block_ends = jnp.einsum(
        "mgs,bsgi->bmgi", end_weights, blocks_in, precision=lax.Precision.HIGHEST
    )
    inner_decay = jnp.exp(-scaled_rates * block_len)[:, :, None]
    running = jnp.zeros((mode_count, filter_count, group_width), jnp.float32)
    starts_list = []
    for block_number in range(block_count):
        starts_list.append(running)
        running = inner_decay * running + block_ends[block_number]
    local_starts = jnp.stack(starts_list, axis=0)
    end_state = running.reshape(mode_count, width_here)
    block_decay = jnp.repeat(jnp.exp(-scaled_rates * rows_here), group_width, axis=1)
    incoming = jnp.zeros((mode_count, width_here), jnp.float32)
    for hop_number in range(lax.axis_size("seq") - 1):
        incoming = passed_along(end_state + block_decay * incoming, "seq", 1)
    block_offsets = (jnp.arange(block_count, dtype=jnp.float32) * block_len)[:, None, None]
    start_decay = jnp.exp(-scaled_rates[None] * block_offsets)
    block_starts = (
        local_starts
        + start_decay[..., None] * incoming.reshape(mode_count, filter_count, group_width)[None]
    )
    carry_weights = residues[None] * jnp.exp(
        -scaled_rates[None] * (offsets_in + 1.0)[:, None, None]
    )
    carried = jnp.einsum(
        "tmg,bmgi->btgi", carry_weights, block_starts, precision=lax.Precision.HIGHEST
    )
    convolved = (local_part + carried).reshape(rows_here, width_here)
    gated_out = (query_stream * convolved).astype(jnp.bfloat16)
    turned = lax.psum_scatter(
        lax.dot_general(
            out_weight, gated_out, (((0,), (1,)), ((), ())), preferred_element_type=jnp.float32
        ),
        "ch",
        scatter_dimension=0,
        tiled=True,
    )
    mixed = turned.T.astype(jnp.bfloat16)
    return mixed


def solution(mesh):
    in_specs = (
        P("seq", "ch"),
        P(None, None, "ch"),
        P(None, None, "ch"),
        P(None, "ch"),
        P(None, "ch"),
        P("ch", None),
    )
    out_specs = P("seq", "ch")
    return jax.shard_map(
        on_device, mesh=mesh, in_specs=in_specs, out_specs=out_specs, check_vma=False
    )
```

profile of v0, /device:TPU:8, one launch (start us, length us, event | category | flops | bytes accessed | tf_op | source)
XLA Modules:
  0.0 342.4 jit_solution(9144535828070933124)
XLA Ops:
  6.5 0.0 copy-start
  6.5 0.0 all-gather.2.cloned.1.call-start
  6.5 0.7 all-gather.2.cloned.1.call-update
  7.3 0.0 copy-start.3
  7.3 0.0 copy-start.2
  7.3 0.0 copy-start.1
  7.3 0.0 reduce-scatter.2.cloned.1.call-start
  7.3 8.8 %copy.18 = bf16[8192,3,128]{0,2,1:T(8,128)(2,1)} copy(bf16[8192,3,128]{2,0,1:T(8,128)(2,1)} %param.7) | data formatting | bytes 12582912 | tf_op args[1]
  16.1 0.0 copy-done.3
  16.1 0.0 copy-done.2
  16.1 0.1 multiply_reduce_fusion
  16.2 0.0 copy-done.1
  16.3 0.1 multiply_exponential_fusion
  16.4 72.4 %all-gather.2.cloned.1.call-done = bf16[256,8192]{1,0:T(8,128)(2,1)} async-done(((bf16[256,128]{1,0:T(8,128)(2,1)}), bf16[256,8192]{1,0:T(8,128)(2,1)}) %all-gather.2.cloned.1.call-update) | async-done | bytes 4194320 | tf_op jit(solution)/shard_map/all_gather | solution.py:25
  88.8 6.4 %convolution_convert_fusion = bf16[256,384]{1,0:T(8,128)(2,1)S(1)} fusion(bf16[256,8192]{1,0:T(8,128)(2,1)} %all-gather.2.cloned.1.call-done, bf16[8192,384]{0,1:T(8,128)(2,1)} %bitcast.77), kind=kOutput, calls=%fused_computation.2 | convolution fusion | flops 1610711040 | bytes 10682368 | tf_op jit(solution)/shard_map/dot_general | solution.py:26
  95.2 3.4 collective-permute-start
  98.6 2.1 collective-permute-done
  100.7 0.1 fusion.4
  100.9 0.1 copy.19
  101.0 0.1 reshape.78
  101.1 0.3 convolution_bitcast_fusion.1
  101.4 3.4 collective-permute-start.1
  104.9 2.7 collective-permute-done.1
  107.6 3.4 collective-permute-start.2
  111.0 0.1 copy.20
  111.1 54.8 %gather_fusion = f32[16384,8]{1,0:T(8,128)} fusion(f32[8,128]{0,1:T(8,128)S(1)} %bitcast.75, s32[16384]{0:T(1024)S(1)} %bitcast_clamp_fusion), kind=kCustom, calls=%fused_computation | custom fusion | bytes 1114112 | tf_op jit(solution)/shard_map/gather | solution.py:50
  165.9 5.1 %copy.21 = f32[128,128,8]{1,0,2:T(8,128)S(1)} copy(f32[128,128,8]{2,1,0:T(8,128)} %bitcast.76) | data formatting | bytes 1048576 | tf_op jit(solution)/shard_map/gather | solution.py:50
  171.0 0.0 collective-permute-done.2
  171.1 3.1 collective-permute-start.3
  174.2 0.9 fusion.1
  175.1 2.1 collective-permute-done.3
  177.2 0.3 fusion
  177.6 0.1 copy.24
  177.7 0.1 copy.25
  177.7 0.0 copy-done
  177.8 4.5 %convolution_bitcast_fusion = f32[8192,256]{0,1:T(8,128)} fusion(bf16[128,8192]{1,0:T(8,128)(2,1)S(1)} %copy-done, f32[256,128]{1,0:T(8,128)S(1)} %copy.25, f32[256,384]{1,0:T(8,128)S(1)} %fusion.4), kind=kOutput, calls=%fused_computation.1 | convolution fusion | flops 536936448 | bytes 10747904 | tf_op jit(solution)/shard_map/dot_general | solution.py:84
  182.2 0.0 reduce-scatter.2.cloned.1.call-update
  182.2 151.8 %reduce-scatter.2.cloned.1.call-done = f32[128,256]{0,1:T(8,128)} async-done(((f32[8192,256]{0,1:T(8,128)}), f32[128,256]{0,1:T(8,128)}) %reduce-scatter.2.cloned.1.call-update) | async-done | bytes 131088 | tf_op jit(solution)/shard_map/reduce_scatter | solution.py:83
  334.1 1.5 convert_bitcast_fusion
  (15 shorter events, 0.2 us)
Async XLA Ops:
  6.5 171.2 %copy-start = (bf16[128,8192]{1,0:T(8,128)(2,1)S(1)}, bf16[128,8192]{1,0:T(8,128)(2,1)}, u32[]{:S(2)}) copy-start(bf16[128,8192]{1,0:T(8,128)(2,1)} %param.11) | copy-start | bytes 6291460
  6.5 82.2 %all-gather.2.cloned.1.call-start = ((), (), s32[]{:S(2)}) async-start(), calls=%async_computation.1 | async-start | bytes 4259840 | tf_op jit(solution)/shard_map/all_gather | solution.py:25
  7.3 8.8 %copy-start.3 = (f32[16,8]{0,1:T(8,128)S(1)}, f32[16,8]{0,1:T(8,128)}, u32[]{:S(2)}) copy-start(f32[16,8]{0,1:T(8,128)} %param.9) | copy-start | bytes 1540
  7.3 8.9 %copy-start.2 = (f32[16,8]{0,1:T(8,128)S(1)}, f32[16,8]{0,1:T(8,128)}, u32[]{:S(2)}) copy-start(f32[16,8]{0,1:T(8,128)} %param.10) | copy-start | bytes 1540
  7.3 9.0 %copy-start.1 = (f32[3,3,128]{2,1,0:T(4,128)S(1)}, f32[3,3,128]{2,1,0:T(4,128)}, u32[]{:S(2)}) copy-start(f32[3,3,128]{2,1,0:T(4,128)} %param.8) | copy-start | bytes 13828
  7.3 326.8 %reduce-scatter.2.cloned.1.call-start = ((), (), s32[]{:S(2)}) async-start(), calls=%async_computation.2 | async-start | bytes 8519680 | tf_op jit(solution)/shard_map/reduce_scatter | solution.py:83
  95.2 5.5 %collective-permute-start = (bf16[2,384]{1,0:T(2,128)(2,1)S(1)}, bf16[2,384]{1,0:T(2,128)(2,1)S(1)}, u32[]{:S(2)}, u32[]{:S(2)}) collective-permute-start(bf16[2,384]{1,0:T(2,128)(2,1)S(1)} %slice.53), channel_id=1, source_target_pairs={{0,64},{64,128},{128,192},{1,65},{65,129},{129,193},{2,66},{66,130... | collective-permute-start | bytes 4616 | tf_op jit(solution)/shard_map/ppermute | solution.py:13
  101.4 6.2 %collective-permute-start.1 = (f32[16,128]{0,1:T(8,128)S(1)}, f32[16,128]{0,1:T(8,128)S(1)}, u32[]{:S(2)}, u32[]{:S(2)}) collective-permute-start(f32[16,128]{0,1:T(8,128)S(1)} %get-tuple-element.5), channel_id=1, source_target_pairs={{0,64},{64,128},{128,192},{1,65},{65,129},{129,193},{2,66},{66,130... | collective-permute-start | bytes 24584 | tf_op jit(solution)/shard_map/ppermute | solution.py:13
  107.6 63.4 %collective-permute-start.2 = (f32[16,128]{0,1:T(8,128)S(1)}, f32[16,128]{0,1:T(8,128)S(1)}, u32[]{:S(2)}, u32[]{:S(2)}) collective-permute-start(f32[16,128]{0,1:T(8,128)S(1)} %fusion.15), channel_id=1, source_target_pairs={{0,64},{64,128},{128,192},{1,65},{65,129},{129,193},{2,66},{66,130... | collective-permute-start | bytes 24584 | tf_op jit(solution)/shard_map/ppermute | solution.py:13
  171.1 6.2 %collective-permute-start.3 = (f32[16,128]{0,1:T(8,128)S(1)}, f32[16,128]{0,1:T(8,128)S(1)}, u32[]{:S(2)}, u32[]{:S(2)}) collective-permute-start(f32[16,128]{0,1:T(8,128)S(1)} %fusion.16), channel_id=1, source_target_pairs={{0,64},{64,128},{128,192},{1,65},{65,129},{129,193},{2,66},{66,130... | collective-permute-start | bytes 24584 | tf_op jit(solution)/shard_map/ppermute | solution.py:13
Sparse Core Ops, SparseCore 0:
  9.9 78.8 all-gather.1
  182.4 151.6 reduce-scatter.1
where the time goes:
time: 343 us; the launch traced here: 342 us
  waiting for transfers between devices  232 us (68%)
  local copies, waits for them, and re-layouts  69.1 us (20%)
  between operations  13.7 us (4%)
  starting transfers between devices  13.3 us (4%)
  matrix products  12.4 us (4%)
    reduce_scatter x1, waiting for transfers between devices, on_device(): lax.psum_scatter(lax.dot_general(out_weight, gated_out, (((0,), (1,)), ((...  152 us
    all_gather x1, waiting for transfers between devices, on_device(): gathered = lax.all_gather(tokens, 'ch', axis=1, tiled=True)  72.4 us
    gather x2, local copies, waits for them, and re-layouts, on_device(): toeplitz = jnp.where((distance >= 0)[None], filter_taps.T[:, lookup], 0.0)  59.9 us
    ppermute x4, starting transfers between devices, passed_along(): return lax.ppermute(block, axis, route)  13.3 us
    unnamed x10, local copies, waits for them, and re-layouts  8.78 us
    ppermute x4, waiting for transfers between devices, passed_along(): return lax.ppermute(block, axis, route)  6.93 us
  transfers between devices with their start and end apart: 6, of which 5 were waited for; matrix products, arithmetic and copies ran while one was open for 20% of the time, Pallas kernels for 0%

commit v1 on v0

--- a/solution.py
+++ b/solution.py
@@ -22,7 +22,15 @@
     group_width = width_here // filter_count
     tokens_all = rows_here * lax.axis_size("seq")
     flat_weight = in_weight.reshape(model_width, 3 * width_here)
-    gathered = lax.all_gather(tokens, "ch", axis=1, tiled=True)
+    gathered = jnp.concatenate(
+        jax.lax.all_to_all(
+            jnp.stack([tokens for _ in range(jax.lax.axis_size("ch"))], axis=0),
+            split_axis=0,
+            axis_name="ch",
+            concat_axis=0,
+        ),
+        axis=1,
+    )
     projected = jnp.dot(gathered, flat_weight, preferred_element_type=jnp.float32).astype(
         jnp.bfloat16
     )

time: 343 us -> 369 us (1.076)
  starting transfers between devices: 13.3 us -> 25.9 us
  waiting for transfers between devices: 232 us -> 242 us
    all_to_all x0 -> x1, waiting for transfers between devices: none -> 86.5 us  [on_device(): jax.lax.all_to_all(jnp.stack([tokens for _ in range(jax.lax.axis_size('ch...]
    all_gather x1 -> x0, waiting for transfers between devices: 72.4 us -> none  [on_device(): gathered = lax.all_gather(tokens, 'ch', axis=1, tiled=True)]
    all_to_all x0 -> x1, starting transfers between devices: none -> 12.2 us  [on_device(): jax.lax.all_to_all(jnp.stack([tokens for _ in range(jax.lax.axis_size('ch...]
    unnamed x10 -> x11, local copies, waits for them, and re-layouts: 8.78 us -> 9.86 us
  transfers between devices with their start and end apart: 6 -> 6, of which waited for: 5 -> 5; matrix products, arithmetic and copies ran while one was open for 20% -> 19% of each run, Pallas kernels for 0% -> 0%
where the time goes in v1:
time: 369 us; the launch traced here: 368 us
  waiting for transfers between devices  242 us (66%)
  local copies, waits for them, and re-layouts  72.4 us (20%)
  starting transfers between devices  25.9 us (7%)
  between operations  13.7 us (4%)
  matrix products  12.5 us (3%)
    reduce_scatter x1, waiting for transfers between devices, on_device(): lax.psum_scatter(lax.dot_general(out_weight, gated_out, (((0,), (1,)), ((...  149 us
    all_to_all x1, waiting for transfers between devices, on_device(): jax.lax.all_to_all(jnp.stack([tokens for _ in range(jax.lax.axis_size('ch...  86.5 us
    gather x2, local copies, waits for them, and re-layouts, on_device(): toeplitz = jnp.where((distance >= 0)[None], filter_taps.T[:, lookup], 0.0)  59.6 us
    ppermute x4, starting transfers between devices, passed_along(): return lax.ppermute(block, axis, route)  13.6 us
    all_to_all x1, starting transfers between devices, on_device(): jax.lax.all_to_all(jnp.stack([tokens for _ in range(jax.lax.axis_size('ch...  12.2 us
    unnamed x11, local copies, waits for them, and re-layouts  9.86 us
  transfers between devices with their start and end apart: 6, of which 5 were waited for; matrix products, arithmetic and copies ran while one was open for 19% of the time, Pallas kernels for 0%

profile of v1, /device:TPU:8, one launch (start us, length us, event | category | flops | bytes accessed | tf_op | source)
XLA Modules:
  0.0 368.5 jit_solution(15761244338320215660)
XLA Ops:
  6.5 0.0 copy-start
  6.5 1.1 copy.19
  7.6 2.6 stack.4
  10.2 12.2 %all-to-all-start = ((bf16[64,256,128]{1,2,0:T(8,128)(2,1)}), bf16[64,256,128]{1,2,0:T(8,128)(2,1)}, u32[]{:S(2)}, u32[]{:S(2)}) async-start(bf16[64,256,128]{1,2,0:T(8,128)(2,1)} %stack.4), calls=%async_computation | async-start | bytes 8388608 | tf_op jit(solution)/shard_map/all_to_all | solution.py:26
  22.4 0.0 copy-start.3
  22.4 0.0 copy-start.2
  22.4 0.0 copy-start.1
  22.4 0.0 reduce-scatter.2.cloned.1.call-start
  22.5 8.7 %copy.20 = bf16[8192,3,128]{0,2,1:T(8,128)(2,1)} copy(bf16[8192,3,128]{2,0,1:T(8,128)(2,1)} %param.7) | data formatting | bytes 12582912 | tf_op args[1]
  31.2 0.0 copy-done.3
  31.3 0.0 copy-done.2
  31.3 0.1 multiply_reduce_fusion
  31.4 0.0 copy-done.1
  31.4 0.1 multiply_exponential_fusion
  31.5 86.5 %all-to-all-done = bf16[64,256,128]{1,2,0:T(8,128)(2,1)} async-done(((bf16[64,256,128]{1,2,0:T(8,128)(2,1)}), bf16[64,256,128]{1,2,0:T(8,128)(2,1)}, u32[]{:S(2)}, u32[]{:S(2)}) %all-to-all-start) | async-done | bytes 4194336 | tf_op jit(solution)/shard_map/all_to_all | solution.py:26
  118.0 6.4 %convolution_convert_fusion = bf16[256,384]{1,0:T(8,128)(2,1)S(1)} fusion(bf16[256,8192]{0,1:T(8,128)(2,1)} %bitcast.2, bf16[8192,384]{0,1:T(8,128)(2,1)} %bitcast.80), kind=kOutput, calls=%fused_computation.2 | convolution fusion | flops 1610711040 | bytes 10682368 | tf_op jit(solution)/shard_map/dot_general | solution.py:34
  124.4 3.5 collective-permute-start
  127.9 2.0 collective-permute-done
  130.0 0.1 fusion.4
  130.1 0.1 copy.21
  130.2 0.1 reshape.88
  130.3 0.3 convolution_bitcast_fusion.1
  130.7 3.5 collective-permute-start.1
  134.2 2.6 collective-permute-done.1
  136.8 3.5 collective-permute-start.2
  140.3 0.1 copy.22
  140.4 54.4 %gather_fusion = f32[16384,8]{1,0:T(8,128)} fusion(f32[8,128]{0,1:T(8,128)S(1)} %bitcast.78, s32[16384]{0:T(1024)S(1)} %bitcast_clamp_fusion), kind=kCustom, calls=%fused_computation | custom fusion | bytes 1114112 | tf_op jit(solution)/shard_map/gather | solution.py:58
  194.9 5.1 %copy.23 = f32[128,128,8]{1,0,2:T(8,128)S(1)} copy(f32[128,128,8]{2,1,0:T(8,128)} %bitcast.79) | data formatting | bytes 1048576 | tf_op jit(solution)/shard_map/gather | solution.py:58
  200.0 0.0 collective-permute-done.2
  200.0 3.2 collective-permute-start.3
  203.2 0.9 fusion.1
  204.2 2.0 collective-permute-done.3
  206.2 0.3 fusion
  206.5 0.1 copy.26
  206.6 0.1 copy.27
  206.7 0.0 copy-done
  206.7 4.5 %convolution_bitcast_fusion = f32[8192,256]{0,1:T(8,128)} fusion(bf16[128,8192]{1,0:T(8,128)(2,1)S(1)} %copy-done, f32[256,128]{1,0:T(8,128)S(1)} %copy.27, f32[256,384]{1,0:T(8,128)S(1)} %fusion.4), kind=kOutput, calls=%fused_computation.1 | convolution fusion | flops 536936448 | bytes 10747904 | tf_op jit(solution)/shard_map/dot_general | solution.py:92
  211.2 0.0 reduce-scatter.2.cloned.1.call-update
  211.2 148.9 %reduce-scatter.2.cloned.1.call-done = f32[128,256]{0,1:T(8,128)} async-done(((f32[8192,256]{0,1:T(8,128)}), f32[128,256]{0,1:T(8,128)}) %reduce-scatter.2.cloned.1.call-update) | async-done | bytes 131088 | tf_op jit(solution)/shard_map/reduce_scatter | solution.py:91
  360.1 1.5 convert_bitcast_fusion
  (15 shorter events, 0.2 us)
Async XLA Ops:
  6.5 200.2 %copy-start = (bf16[128,8192]{1,0:T(8,128)(2,1)S(1)}, bf16[128,8192]{1,0:T(8,128)(2,1)}, u32[]{:S(2)}) copy-start(bf16[128,8192]{1,0:T(8,128)(2,1)} %param.11) | copy-start | bytes 6291460
  10.2 107.8 %all-to-all-start = ((bf16[64,256,128]{1,2,0:T(8,128)(2,1)}), bf16[64,256,128]{1,2,0:T(8,128)(2,1)}, u32[]{:S(2)}, u32[]{:S(2)}) async-start(bf16[64,256,128]{1,2,0:T(8,128)(2,1)} %stack.4), calls=%async_computation | async-start | bytes 8388608 | tf_op jit(solution)/shard_map/all_to_all | solution.py:26
  22.4 8.8 %copy-start.3 = (f32[16,8]{0,1:T(8,128)S(1)}, f32[16,8]{0,1:T(8,128)}, u32[]{:S(2)}) copy-start(f32[16,8]{0,1:T(8,128)} %param.9) | copy-start | bytes 1540
  22.4 8.8 %copy-start.2 = (f32[16,8]{0,1:T(8,128)S(1)}, f32[16,8]{0,1:T(8,128)}, u32[]{:S(2)}) copy-start(f32[16,8]{0,1:T(8,128)} %param.10) | copy-start | bytes 1540
  22.4 9.0 %copy-start.1 = (f32[3,3,128]{2,1,0:T(4,128)S(1)}, f32[3,3,128]{2,1,0:T(4,128)}, u32[]{:S(2)}) copy-start(f32[3,3,128]{2,1,0:T(4,128)} %param.8) | copy-start | bytes 13828
  22.4 337.6 %reduce-scatter.2.cloned.1.call-start = ((), (), s32[]{:S(2)}) async-start(), calls=%async_computation.2 | async-start | bytes 8519680 | tf_op jit(solution)/shard_map/reduce_scatter | solution.py:91
  124.4 5.5 %collective-permute-start = (bf16[2,384]{1,0:T(2,128)(2,1)S(1)}, bf16[2,384]{1,0:T(2,128)(2,1)S(1)}, u32[]{:S(2)}, u32[]{:S(2)}) collective-permute-start(bf16[2,384]{1,0:T(2,128)(2,1)S(1)} %slice.53), channel_id=1, source_target_pairs={{0,64},{64,128},{128,192},{1,65},{65,129},{129,193},{2,66},{66,130... | collective-permute-start | bytes 4616 | tf_op jit(solution)/shard_map/ppermute | solution.py:13
  130.7 6.2 %collective-permute-start.1 = (f32[16,128]{0,1:T(8,128)S(1)}, f32[16,128]{0,1:T(8,128)S(1)}, u32[]{:S(2)}, u32[]{:S(2)}) collective-permute-start(f32[16,128]{0,1:T(8,128)S(1)} %get-tuple-element.5), channel_id=1, source_target_pairs={{0,64},{64,128},{128,192},{1,65},{65,129},{129,193},{2,66},{66,130... | collective-permute-start | bytes 24584 | tf_op jit(solution)/shard_map/ppermute | solution.py:13
  136.8 63.2 %collective-permute-start.2 = (f32[16,128]{0,1:T(8,128)S(1)}, f32[16,128]{0,1:T(8,128)S(1)}, u32[]{:S(2)}, u32[]{:S(2)}) collective-permute-start(f32[16,128]{0,1:T(8,128)S(1)} %fusion.15), channel_id=1, source_target_pairs={{0,64},{64,128},{128,192},{1,65},{65,129},{129,193},{2,66},{66,130... | collective-permute-start | bytes 24584 | tf_op jit(solution)/shard_map/ppermute | solution.py:13
  200.0 6.2 %collective-permute-start.3 = (f32[16,128]{0,1:T(8,128)S(1)}, f32[16,128]{0,1:T(8,128)S(1)}, u32[]{:S(2)}, u32[]{:S(2)}) collective-permute-start(f32[16,128]{0,1:T(8,128)S(1)} %fusion.16), channel_id=1, source_target_pairs={{0,64},{64,128},{128,192},{1,65},{65,129},{129,193},{2,66},{66,130... | collective-permute-start | bytes 24584 | tf_op jit(solution)/shard_map/ppermute | solution.py:13
Sparse Core Ops, SparseCore 0:
  211.3 148.6 reduce-scatter.1
